TPU v7x, 512 devices: a whole 4x4x16 slice. The times are simulated.
512 devices in a mesh: dp: 4 (over x), seq: 8 (over z_lo), tensor: 16 (over z_hi, y, core).
Axes of the slice: x: 4, y: 4, z: 16 (z_hi: 2, z_lo: 8; z = z_hi * 8 + z_lo), core: 2. Of those that a mesh axis runs over, the one named last changes fastest.
Arguments:
- features: bfloat16 [4096, 4096], P(('dp', 'seq'), 'tensor'), parts along dimension 0, may hold values from -6 to 6
- in_weight: bfloat16 [4096, 3, 4096], P('seq', None, 'tensor'), may hold values from -0.09375 to 0.09375
- short_taps: float32 [3, 7, 4096], P(None, None, 'tensor'), may hold values from -2.5 to 2.5
- decay_rates: float32 [16, 4096], P(None, 'tensor'), may hold values from 0.00048828125 to 0.1
- residues: float32 [16, 4096], P(None, 'tensor'), may hold values from -1.5 to 1.5
- skip_gain: float32 [4096], P('tensor'), may hold values from 0.5 to 1.5
- out_weight: bfloat16 [4096, 4096], P(None, 'tensor'), may hold values from -0.09375 to 0.09375
Outputs:
- mixed: bfloat16 [4096, 4096], P(('dp', 'seq'), 'tensor'), parts along dimension 0
There are 4 independent parts, one for each index of `dp`. A program takes and returns all parts, laid end to end along the dimension named above; an argument that names none is the same for every part. Nothing has to cross between parts.
All inputs are finite; a program needn't handle non-finite values.
Results may differ from a plain program's by a relative error of at most 0.007.
Values may be sent and summed in bfloat16 or wider, within the bound.
No kernel may reach another device: no remote copies, remote signals or barrier semaphores. Data moves between devices by JAX's collectives and lax.ppermute only.
A program may use at most 64 MiB of HBM per device.

v0:
```python
import jax
import jax.numpy as jnp
from jax import lax
from jax.sharding import PartitionSpec as P

precise = lax.Precision.HIGHEST
block_len = 64


def passed_along(value, axis, steps):
    count = lax.axis_size(axis)
    leading, last = (max(0, -steps), min(count, count - steps))
    return lax.ppermute(value, axis, [(source, source + steps) for source in range(leading, last)])


def prefix_2(part, axis, combine, identity):
    place = lax.axis_index(axis)
    gathered = jax.tree.map(lambda a: lax.all_gather(a, axis), part)
    state = jax.tree.map(lambda a, e: jnp.zeros_like(a) + jnp.asarray(e, a.dtype), part, identity)

    def one(turn, state):
        return combine(
            state, jax.tree.map(lambda a: lax.dynamic_index_in_dim(a, turn, 0, False), gathered)
        )

    return lax.fori_loop(0, place, one, state)


def body(features, in_weight, short_taps, decay_rates, residues, skip_gain, out_weight):
    tok_rows = features.shape[0]
    channels = in_weight.shape[2]
    taps_count = short_taps.shape[1]
    whole_feats = lax.all_gather(features, "tensor", axis=1, tiled=True)
    piece = lax.all_gather(in_weight, "seq", axis=0, tiled=True)
    count = piece.shape[0]
    projected = jnp.dot(
        whole_feats, piece.reshape(count, 3 * channels), preferred_element_type=jnp.float32
    )
    projected = projected.astype(jnp.bfloat16).reshape(tok_rows, 3, channels)
    rim_rows = taps_count - 1
    earlier = passed_along(projected[tok_rows - rim_rows :], "seq", 1)
    extended = jnp.concatenate([earlier, projected], axis=0).astype(jnp.float32)
    short = jnp.zeros((tok_rows, 3, channels), jnp.float32)
    for offset_lag in range(taps_count):
        short = (
            short
            + short_taps[:, offset_lag, :][None]
            * extended[rim_rows - offset_lag : rim_rows - offset_lag + tok_rows]
        )
    product = short[:, 1, :] * short[:, 2, :]
    blocks = tok_rows // block_len
    pieces = product.reshape(blocks, block_len, channels)
    amplitude = residues * jnp.sqrt(2.0 * decay_rates)
    offsets = jnp.arange(block_len).astype(jnp.float32)
    falloff = jnp.exp(-decay_rates[:, None, :] * offsets[None, :, None])
    kernel = jnp.einsum("mc,mtc->tc", amplitude, falloff, precision=precise)
    lag_grid = jnp.arange(block_len)[:, None] - jnp.arange(block_len)[None, :]
    select = (lag_grid[:, :, None] == jnp.arange(block_len)[None, None, :]).astype(jnp.float32)
    toeplitz = jnp.einsum("tsk,kc->tsc", select, kernel, precision=precise)
    inner = jnp.einsum("tsc,bsc->btc", toeplitz, pieces, precision=precise)
    toward_end = jnp.exp(-decay_rates[:, None, :] * (block_len - offsets)[None, :, None])
    block_sums = jnp.einsum("msc,bsc->bmc", toward_end, pieces, precision=precise)
    block_index = jnp.arange(blocks).astype(jnp.float32)
    carry_over = jnp.exp(
        -decay_rates[None] * (block_len * (blocks - 1 - block_index))[:, None, None]
    )
    device_sum = jnp.sum(carry_over * block_sums, axis=0)
    device_decay = jnp.exp(-decay_rates * float(tok_rows))

    def combine(earlier_pair, later_pair):
        return (earlier_pair[0] * later_pair[0], later_pair[0] * earlier_pair[1] + later_pair[1])

    prefix = prefix_2(
        (device_decay, device_sum),
        "seq",
        combine,
        (jnp.ones_like(device_decay), jnp.zeros_like(device_sum)),
    )
    entering = prefix[1]
    step_decay = jnp.exp(-decay_rates * float(block_len))

    def advance(state, block_sum):
        return (step_decay * state + block_sum, state)

    final_state, starts = lax.scan(advance, entering, block_sums)
    outer = jnp.einsum("mic,bmc->bic", amplitude[:, None, :] * falloff, starts, precision=precise)
    conv = (inner + outer).reshape(tok_rows, channels)
    gated = (short[:, 0, :] * (conv + skip_gain[None, :] * product)).astype(jnp.bfloat16)
    mixed = jnp.dot(
        lax.all_gather(gated, "tensor", axis=1, tiled=True),
        out_weight,
        preferred_element_type=jnp.float32,
    )
    return mixed.astype(jnp.bfloat16)


def solution(mesh):
    in_specs = (
        P(("dp", "seq"), "tensor"),
        P("seq", None, "tensor"),
        P(None, None, "tensor"),
        P(None, "tensor"),
        P(None, "tensor"),
        P("tensor"),
        P(None, "tensor"),
    )
    out_specs = P(("dp", "seq"), "tensor")
    return jax.shard_map(body, mesh=mesh, in_specs=in_specs, out_specs=out_specs, check_vma=False)
```

profile of v0, /device:TPU:1, one launch (start us, length us, event | category | flops | bytes accessed | tf_op | source)
XLA Modules:
  0.0 453.0 jit_solution(18063631675276910231)
XLA Ops:
  6.5 0.0 copy-start
  6.5 0.0 all-gather.6.cloned.1.call-start
  6.6 0.7 all-gather.6.cloned.1.call-update
  7.3 0.0 all-gather.8.cloned.1.call-start
  7.3 2.3 copy.59
  9.7 0.0 all-gather.8.cloned.1.call-update
  9.7 0.0 all-gather.10.cloned.1.call-start
  9.7 0.0 copy-done.4
  9.7 0.0 copy-done.5
  9.8 0.1 copy.90
  9.9 0.1 copy.63
  10.0 0.0 copy-start.7
  10.0 0.5 subtract_multiply_fusion
  10.5 0.5 broadcast_subtract_fusion
  11.1 1.6 multiply_reduce_fusion
  12.7 0.0 copy-done.3
  12.8 3.8 fusion.5
  16.6 76.7 %all-gather.6.cloned.1.call-done = bf16[128,4096]{1,0:T(8,128)(2,1)} async-done(((bf16[128,256]{1,0:T(8,128)(2,1)}), bf16[128,4096]{1,0:T(8,128)(2,1)}) %all-gather.6.cloned.1.call-update) | async-done | bytes 1048592 | tf_op jit(solution)/shard_map/all_gather | solution.py:33
  93.3 135.5 %all-gather.8.cloned.1.call-done = bf16[4096,3,256]{0,2,1:T(8,128)(2,1)} async-done(((bf16[512,3,256]{0,2,1:T(8,128)(2,1)}), bf16[4096,3,256]{0,2,1:T(8,128)(2,1)}) %all-gather.8.cloned.1.call-update) | async-done | bytes 6291472 | tf_op jit(solution)/shard_map/all_gather | solution.py:34
  228.8 5.3 %convolution_convert_fusion = bf16[128,768]{1,0:T(8,128)(2,1)S(1)} fusion(bf16[128,4096]{1,0:T(8,128)(2,1)} %all-gather.6.cloned.1.call-done, bf16[4096,768]{0,1:T(8,128)(2,1)} %bitcast.70), kind=kOutput, calls=%fused_computation.13 | convolution fusion | flops 805404672 | bytes 7536640 | tf_op jit(solution)/shard_map/dot_general | solution.py:36
  234.2 0.2 copy.81
  234.4 1.3 collective-permute-start
  235.7 40.2 %all-gather = f32[128,256]{1,0:T(8,128)S(1)} all-gather(f32[16,256]{1,0:T(8,128)S(1)} %get-tuple-element.136), channel_id=2, replica_groups=mesh['dp'=4,'seq'=8,'tensor'=16] {'seq'}, dimensions={0}, use_global_device_ids=true | all-gather | bytes 147456 | tf_op jit(solution)/shard_map/all_gather | solution.py:18
  275.8 0.8 copy.70
  276.6 9.2 %copy.65 = f32[64,64,256]{1,0,2:T(8,128)} copy(f32[64,64,256]{2,1,0:T(8,128)} %fusion.5) | data formatting | bytes 8388608 | tf_op jit(solution)/shard_map/tsk,kc->tsc/dot_general | solution.py:59
  285.8 0.2 copy.61
  285.9 0.0 collective-permute-done
  285.9 0.2 maximum_convert_fusion
  286.1 1.5 fusion.21
  287.6 0.1 copy.62
  287.8 0.1 copy.64
  287.9 15.4 %fusion.32 = f32[256,2,64]{2,1,0:T(2,128)S(1)} fusion(f32[2,64,256]{1,0,2:T(2,128)S(1)} %copy.64, f32[64,64,256]{1,0,2:T(8,128)} %copy.65), kind=kOutput, calls=%fused_computation.61 | convolution fusion | flops 25165824 | bytes 4456448 | tf_op jit(solution)/shard_map/tsc,bsc->btc/dot_general | solution.py:60
  303.4 4.2 multiply_reduce_fusion.1
  307.6 1.0 copy.68
  308.6 39.9 %all-gather.1 = f32[128,256]{1,0:T(8,128)S(1)} all-gather(f32[16,256]{1,0:T(8,128)S(1)} %copy.68), channel_id=3, replica_groups=mesh['dp'=4,'seq'=8,'tensor'=16] {'seq'}, dimensions={0}, use_global_device_ids=true | all-gather | bytes 147456 | tf_op jit(solution)/shard_map/all_gather | solution.py:18
  348.5 0.1 copy.69
  348.6 1.2 while.25
  348.6 0.6 bitcast_dynamic-update-slice_fusion.2
  349.2 0.6 bitcast_dynamic-update-slice_fusion.2
  349.8 0.9 copy.71
  350.7 0.0 copy-start.6
  350.7 3.7 fusion.12
  354.5 0.1 copy.72
  354.6 0.1 copy.73
  354.7 0.7 fusion.28
  355.5 0.0 all-gather.10.cloned.1.call-update
  355.5 88.6 %all-gather.10.cloned.1.call-done = bf16[128,4096]{0,1:T(8,128)(2,1)} async-done(((bf16[128,256]{0,1:T(8,128)(2,1)}), bf16[128,4096]{0,1:T(8,128)(2,1)}) %all-gather.10.cloned.1.call-update) | async-done | bytes 1048592 | tf_op jit(solution)/shard_map/all_gather | solution.py:90
  444.1 2.4 convolution_convert_fusion.1
  (29 shorter events, 0.1 us)
Async XLA Ops:
  6.5 437.5 %copy-start = (bf16[4096,256]{1,0:T(8,128)(2,1)S(1)}, bf16[4096,256]{1,0:T(8,128)(2,1)}, u32[]{:S(2)}) copy-start(bf16[4096,256]{1,0:T(8,128)(2,1)} %param.17) | copy-start | bytes 6291460
  6.5 3.2 copy-start.4
  6.5 3.2 copy-start.5
  6.5 6.2 %copy-start.3 = (f32[3,7,256]{2,1,0:T(8,128)S(1)}, f32[3,7,256]{2,1,0:T(8,128)}, u32[]{:S(2)}) copy-start(f32[3,7,256]{2,1,0:T(8,128)} %param.13) | copy-start | bytes 64516
  6.5 86.7 %all-gather.6.cloned.1.call-start = ((), (), s32[]{:S(2)}) async-start(), calls=%async_computation | async-start | bytes 1114112 | tf_op jit(solution)/shard_map/all_gather | solution.py:33
  7.3 221.5 %all-gather.8.cloned.1.call-start = ((), (), s32[]{:S(2)}) async-start(), calls=%async_computation.1 | async-start | bytes 7077888 | tf_op jit(solution)/shard_map/all_gather | solution.py:34
  9.7 434.4 %all-gather.10.cloned.1.call-start = ((), (), s32[]{:S(2)}) async-start(), calls=%async_computation.2 | async-start | bytes 1114112 | tf_op jit(solution)/shard_map/all_gather | solution.py:90
  10.0 6.6 %copy-start.1 = (f32[16,256]{0,1:T(8,128)}, f32[16,256]{0,1:T(8,128)S(1)}, u32[]{:S(2)}) copy-start(f32[16,256]{0,1:T(8,128)S(1)} %copy.63) | copy-start | bytes 49156
  10.0 6.6 %copy-start.7 = (f32[64]{0:T(128)}, f32[64]{0:T(128)S(1)}, u32[]{:S(2)}) copy-start(f32[64]{0:T(128)S(1)} %iota_convert_fusion) | copy-start | bytes 772
  234.4 51.6 %collective-permute-start = (bf16[6,3,256]{0,2,1:T(8,128)(2,1)S(1)}, bf16[6,3,256]{0,2,1:T(8,128)(2,1)S(1)}, u32[]{:S(2)}, u32[]{:S(2)}) collective-permute-start(bf16[6,3,256]{0,2,1:T(8,128)(2,1)S(1)} %bitcast.76), channel_id=1, source_target_pairs={{0,16},{16,32},{32,48},{48,64},{64,80},{80,96},{96,112},{1,17},{17... | collective-permute-start | bytes 27656 | tf_op jit(solution)/shard_map/ppermute | solution.py:13
  287.9 15.5 %copy-start.2 = (f32[16,256]{0,1:T(8,128)S(1)}, f32[16,256]{0,1:T(8,128)}, u32[]{:S(2)}) copy-start(f32[16,256]{0,1:T(8,128)} %copy-done.1) | copy-start | bytes 49156
  287.9 15.4 %copy-start.8 = (f32[2]{0:T(128)S(1)}, f32[2]{0:T(128)}, u32[]{:S(2)}) copy-start(f32[2]{0:T(128)} %subtract_multiply_fusion) | copy-start | bytes 28
  287.9 15.4 %copy-start.9 = (f32[64]{0:T(128)S(1)}, f32[64]{0:T(128)}, u32[]{:S(2)}) copy-start(f32[64]{0:T(128)} %broadcast_subtract_fusion) | copy-start | bytes 772
  350.7 4.0 copy-start.6
Sparse Core Ops, SparseCore 0:
  10.5 82.7 all-gather.5
  95.4 133.4 all-gather.7
  355.6 88.4 all-gather.9
where the time goes:
time: 453 us
  waiting for transfers between devices  301 us (66%)
  blocking collectives  80.1 us (18%)
  matrix products  35 us (8%)
  local copies, waits for them, and re-layouts  16.5 us (4%)
  between operations  13.4 us (3%)
  other arithmetic  5.16 us (1%)
    all_gather x1, waiting for transfers between devices, body(): piece = lax.all_gather(in_weight, 'seq', axis=0, tiled=True)  136 us
    all_gather x1, waiting for transfers between devices, body(): lax.all_gather(gated, 'tensor', axis=1, tiled=True)  88.6 us
    all_gather x2, blocking collectives, prefix_2(): gathered = jax.tree.map(lambda a: lax.all_gather(a, axis), part)  80.1 us
    all_gather x1, waiting for transfers between devices, body(): whole_feats = lax.all_gather(features, 'tensor', axis=1, tiled=True)  76.7 us
    dot_general x1, matrix products, body(): inner = jnp.einsum('tsc,bsc->btc', toeplitz, pieces, precision=precise)  15.4 us
    dot_general x1, local copies, waits for them, and re-layouts, body(): toeplitz = jnp.einsum('tsk,kc->tsc', select, kernel, precision=precise)  9.17 us
  transfers between devices with their start and end apart: 4, of which 3 were waited for; matrix products, arithmetic and copies ran while one was open for 4% of the time, Pallas kernels for 0%

commit v1 on v0

--- a/solution.py
+++ b/solution.py
@@ -31,7 +31,9 @@
     channels = in_weight.shape[2]
     taps_count = short_taps.shape[1]
     whole_feats = lax.all_gather(features, "tensor", axis=1, tiled=True)
-    piece = lax.all_gather(in_weight, "seq", axis=0, tiled=True)
+    piece = jnp.concatenate(
+        lax.all_to_all(jnp.stack(lax.psum(1, "seq") * [in_weight]), "seq", 0, 0), 0
+    )
     count = piece.shape[0]
     projected = jnp.dot(
         whole_feats, piece.reshape(count, 3 * channels), preferred_element_type=jnp.float32

time: 453 us -> 551 us (1.22)
  waiting for transfers between devices: 301 us -> 372 us
  local copies, waits for them, and re-layouts: 16.5 us -> 30.3 us
  starting transfers between devices: 1.42 us -> 14.6 us
    all_to_all x0 -> x1, waiting for transfers between devices: none -> 283 us  [body(): lax.all_to_all(jnp.stack(lax.psum(1, 'seq') * [in_weight]), 'seq', 0, 0)]
    all_gather x1 -> x0, waiting for transfers between devices: 136 us -> none  [body(): piece = lax.all_gather(in_weight, 'seq', axis=0, tiled=True)]
    all_gather x1, waiting for transfers between devices: 76.7 us -> 0.01 us  [body(): whole_feats = lax.all_gather(features, 'tensor', axis=1, tiled=True)]
    all_to_all x0 -> x1, starting transfers between devices: none -> 13.2 us  [body(): lax.all_to_all(jnp.stack(lax.psum(1, 'seq') * [in_weight]), 'seq', 0, 0)]
    all_to_all x0 -> x1, local copies, waits for them, and re-layouts: none -> 6.35 us  [body(): lax.all_to_all(jnp.stack(lax.psum(1, 'seq') * [in_weight]), 'seq', 0, 0)]
    unnamed x26 -> x17, local copies, waits for them, and re-layouts: 2.49 us -> 8.53 us
  transfers between devices with their start and end apart: 4 -> 4, of which waited for: 3 -> 2; matrix products, arithmetic and copies ran while one was open for 4% -> 5% of each run, Pallas kernels for 0% -> 0%
where the time goes in v1:
time: 551 us; the launch traced here: 550 us
  waiting for transfers between devices  372 us (68%)
  blocking collectives  80.1 us (15%)
  matrix products  34.9 us (6%)
  local copies, waits for them, and re-layouts  30.3 us (5%)
  starting transfers between devices  14.6 us (3%)
  between operations  13.6 us (2%)
    all_to_all x1, waiting for transfers between devices, body(): lax.all_to_all(jnp.stack(lax.psum(1, 'seq') * [in_weight]), 'seq', 0, 0)  283 us
    all_gather x1, waiting for transfers between devices, body(): lax.all_gather(gated, 'tensor', axis=1, tiled=True)  89.2 us
    all_gather x2, blocking collectives, prefix_2(): gathered = jax.tree.map(lambda a: lax.all_gather(a, axis), part)  80.1 us
    dot_general x1, matrix products, body(): inner = jnp.einsum('tsc,bsc->btc', toeplitz, pieces, precision=precise)  15.4 us
    all_to_all x1, starting transfers between devices, body(): lax.all_to_all(jnp.stack(lax.psum(1, 'seq') * [in_weight]), 'seq', 0, 0)  13.2 us
  transfers between devices with their start and end apart: 4, of which 2 were waited for; matrix products, arithmetic and copies ran while one was open for 5% of the time, Pallas kernels for 0%

profile of v1, /device:TPU:1, one launch (start us, length us, event | category | flops | bytes accessed | tf_op | source)
XLA Modules:
  0.0 550.1 jit_solution(12459044475568966472)
XLA Ops:
  6.5 0.0 copy-start
  6.5 1.6 copy.62
  8.1 3.3 stack.2
  11.4 0.0 copy-start.2
  11.4 0.0 copy-start.3
  11.4 13.2 %all-to-all-start = ((bf16[8,512,3,256]{1,3,2,0:T(8,128)(2,1)}), bf16[8,512,3,256]{1,3,2,0:T(8,128)(2,1)}, u32[]{:S(2)}, u32[]{:S(2)}) async-start(bf16[8,512,3,256]{1,3,2,0:T(8,128)(2,1)} %stack.2), calls=%async_computation | async-start | bytes 12582912 | tf_op jit(solution)/shard_map/all_to_all | solution.py:35
  24.6 0.0 all-gather.5.cloned.1.call-start
  24.7 0.7 all-gather.5.cloned.1.call-update
  25.4 0.0 all-gather.7.cloned.1.call-start
  25.4 0.0 copy-done.2
  25.4 0.0 copy-done.3
  25.5 0.1 copy.94
  25.6 0.1 copy.67
  25.7 1.6 multiply_reduce_fusion
  27.3 0.0 copy-done.1
  27.4 3.8 fusion.5
  31.2 282.6 %all-to-all-done = bf16[8,512,3,256]{1,3,2,0:T(8,128)(2,1)} async-done(((bf16[8,512,3,256]{1,3,2,0:T(8,128)(2,1)}), bf16[8,512,3,256]{1,3,2,0:T(8,128)(2,1)}, u32[]{:S(2)}, u32[]{:S(2)}) %all-to-all-start) | async-done | bytes 6291488 | tf_op jit(solution)/shard_map/all_to_all | solution.py:35
  313.8 6.4 %copy.63 = bf16[8,512,3,256]{1,0,3,2:T(8,128)(2,1)S(1)} copy(bf16[8,512,3,256]{1,3,2,0:T(8,128)(2,1)} %all-to-all-done) | data formatting | bytes 12582912 | tf_op jit(solution)/shard_map/all_to_all | solution.py:35
  320.1 6.8 %copy.95 = bf16[96,8,8,512]{3,1,2,0:T(8,128)(2,1)} copy(bf16[96,8,8,512]{3,2,1,0:T(8,128)(2,1)S(1)} %bitcast.75) | data formatting | bytes 12582912
  327.0 5.3 convolution_convert_fusion
  332.3 0.2 copy.85
  332.5 1.3 collective-permute-start
  333.8 40.2 %all-gather = f32[128,256]{1,0:T(8,128)S(1)} all-gather(f32[16,256]{1,0:T(8,128)S(1)} %get-tuple-element.136), channel_id=2, replica_groups=mesh['dp'=4,'seq'=8,'tensor'=16] {'seq'}, dimensions={0}, use_global_device_ids=true | all-gather | bytes 147456 | tf_op jit(solution)/shard_map/all_gather | solution.py:18
  374.0 0.7 copy.74
  374.7 9.2 %copy.69 = f32[64,64,256]{1,0,2:T(8,128)} copy(f32[64,64,256]{2,1,0:T(8,128)} %fusion.5) | data formatting | bytes 8388608 | tf_op jit(solution)/shard_map/tsk,kc->tsc/dot_general | solution.py:61
  383.9 0.2 copy.65
  384.1 0.0 collective-permute-done
  384.1 0.2 maximum_convert_fusion
  384.3 1.5 fusion.21
  385.8 0.1 copy.66
  385.9 0.1 copy.68
  386.0 15.4 %fusion.32 = f32[256,2,64]{2,1,0:T(2,128)S(1)} fusion(f32[2,64,256]{1,0,2:T(2,128)S(1)} %copy.68, f32[64,64,256]{1,0,2:T(8,128)} %copy.69), kind=kOutput, calls=%fused_computation.61 | convolution fusion | flops 25165824 | bytes 4456448 | tf_op jit(solution)/shard_map/tsc,bsc->btc/dot_general | solution.py:62
  401.4 4.3 multiply_reduce_fusion.1
  405.7 0.1 copy.72
  405.7 39.9 %all-gather.1 = f32[128,256]{1,0:T(8,128)S(1)} all-gather(f32[16,256]{1,0:T(8,128)S(1)} %copy.72), channel_id=3, replica_groups=mesh['dp'=4,'seq'=8,'tensor'=16] {'seq'}, dimensions={0}, use_global_device_ids=true | all-gather | bytes 147456 | tf_op jit(solution)/shard_map/all_gather | solution.py:18
  445.7 1.0 copy.73
  446.7 0.1 while.25
  446.8 0.1 copy.75
  446.9 0.0 copy-start.4
  447.0 3.7 fusion.12
  450.7 0.1 copy.76
  450.8 0.1 copy.77
  450.9 0.0 copy-done.4
  450.9 0.7 fusion.28
  451.6 0.0 all-gather.7.cloned.1.call-update
  451.7 89.2 %all-gather.7.cloned.1.call-done = bf16[128,4096]{0,1:T(8,128)(2,1)} async-done(((bf16[128,256]{0,1:T(8,128)(2,1)}), bf16[128,4096]{0,1:T(8,128)(2,1)}) %all-gather.7.cloned.1.call-update) | async-done | bytes 1048592 | tf_op jit(solution)/shard_map/all_gather | solution.py:92
  540.9 0.0 copy-done
  540.9 2.4 convolution_convert_fusion.1
  (21 shorter events, 0.1 us)
Async XLA Ops:
  6.5 534.3 %copy-start = (bf16[4096,256]{1,0:T(8,128)(2,1)S(1)}, bf16[4096,256]{1,0:T(8,128)(2,1)}, u32[]{:S(2)}) copy-start(bf16[4096,256]{1,0:T(8,128)(2,1)} %param.17) | copy-start | bytes 6291460
  11.4 14.0 %copy-start.2 = (f32[16,256]{1,0:T(8,128)S(1)}, f32[16,256]{1,0:T(8,128)}, u32[]{:S(2)}) copy-start(f32[16,256]{1,0:T(8,128)} %param.14) | copy-start | bytes 49156
  11.4 14.0 %copy-start.3 = (f32[16,256]{1,0:T(8,128)S(1)}, f32[16,256]{1,0:T(8,128)}, u32[]{:S(2)}) copy-start(f32[16,256]{1,0:T(8,128)} %param.15) | copy-start | bytes 49156
  11.4 15.9 %copy-start.1 = (f32[3,7,256]{2,1,0:T(8,128)S(1)}, f32[3,7,256]{2,1,0:T(8,128)}, u32[]{:S(2)}) copy-start(f32[3,7,256]{2,1,0:T(8,128)} %param.13) | copy-start | bytes 64516
  11.4 302.4 %all-to-all-start = ((bf16[8,512,3,256]{1,3,2,0:T(8,128)(2,1)}), bf16[8,512,3,256]{1,3,2,0:T(8,128)(2,1)}, u32[]{:S(2)}, u32[]{:S(2)}) async-start(bf16[8,512,3,256]{1,3,2,0:T(8,128)(2,1)} %stack.2), calls=%async_computation | async-start | bytes 12582912 | tf_op jit(solution)/shard_map/all_to_all | solution.py:35
  24.6 302.3 %all-gather.5.cloned.1.call-start = ((), (), s32[]{:S(2)}) async-start(), calls=%async_computation.1 | async-start | bytes 1114112 | tf_op jit(solution)/shard_map/all_gather | solution.py:33
  25.4 515.5 %all-gather.7.cloned.1.call-start = ((), (), s32[]{:S(2)}) async-start(), calls=%async_computation.2 | async-start | bytes 1114112 | tf_op jit(solution)/shard_map/all_gather | solution.py:92
  332.5 51.6 %collective-permute-start = (bf16[6,3,256]{0,2,1:T(8,128)(2,1)S(1)}, bf16[6,3,256]{0,2,1:T(8,128)(2,1)S(1)}, u32[]{:S(2)}, u32[]{:S(2)}) collective-permute-start(bf16[6,3,256]{0,2,1:T(8,128)(2,1)S(1)} %bitcast.81), channel_id=1, source_target_pairs={{0,16},{16,32},{32,48},{48,64},{64,80},{80,96},{96,112},{1,17},{17... | collective-permute-start | bytes 27656 | tf_op jit(solution)/shard_map/ppermute | solution.py:13
  446.9 3.9 copy-start.4
Sparse Core Ops, SparseCore 0:
  28.6 139.4 all-gather.4
  451.8 89.0 all-gather.6
